TPU v7x, 512 devices: a whole 4x8x8 slice. The times are simulated.
512 devices in a mesh: chain: 64 (over y, z), cross: 8 (over x, core).
Axes of the slice: x: 4, y: 8, z: 8, core: 2. Of those that a mesh axis runs over, the one named last changes fastest.
Arguments:
- right_side: bfloat16 [64, 1024, 512], P('chain', 'cross'), may hold values from -6 to 6
- self_factor: bfloat16 [6, 64, 1024, 1024], P(None, 'chain', 'cross')
- lower_factor: bfloat16 [6, 64, 1024, 1024], P(None, 'chain', 'cross'), may hold values from -0.078125 to 0.078125
- upper_factor: bfloat16 [6, 64, 1024, 1024], P(None, 'chain', 'cross'), may hold values from -0.078125 to 0.078125
Outputs:
- solution: bfloat16 [64, 1024, 512], P('chain', 'cross')
All inputs are finite; a program needn't handle non-finite values.
Results may differ from a plain program's by a relative error of at most 0.014.
Values may be sent and summed in bfloat16 or wider, within the bound.
No kernel may reach another device: no remote copies, remote signals or barrier semaphores. Data moves between devices by JAX's collectives and lax.ppermute only.
A program may use at most 64 MiB of HBM per device.

v0:
```python
import jax
import jax.numpy as jnp
from jax import lax
from jax.sharding import PartitionSpec as P


def shifted(value, axis, steps):
    count = lax.axis_size(axis)
    initial, last = (max(0, -steps), min(count, count - steps))
    return lax.ppermute(value, axis, [(source, source + steps) for source in range(initial, last)])


def reach_full(piece, dist):
    lower = shifted(piece, "chain", dist)
    upper = shifted(piece, "chain", -dist)
    return (lower, upper)


def body(right_side, self_factor, lower_factor, upper_factor):
    levels = lax.axis_size("chain").bit_length() - 1
    current = right_side[0]
    for level in range(levels):
        dist = 2**level
        own_mat = self_factor[level, 0]
        low_mat = lower_factor[level, 0]
        up_mat = upper_factor[level, 0]
        whole = lax.all_gather(current, "cross", axis=0, tiled=True)
        lower, upper = reach_full(whole, dist)
        total = jnp.dot(own_mat, whole, preferred_element_type=jnp.float32)
        total = total - jnp.dot(low_mat, lower, preferred_element_type=jnp.float32)
        total = total - jnp.dot(up_mat, upper, preferred_element_type=jnp.float32)
        current = total.astype(jnp.bfloat16)
    return current[None]


def solution(mesh):
    return jax.shard_map(
        body,
        mesh=mesh,
        in_specs=(
            P("chain", "cross", None),
            P(None, "chain", "cross", None),
            P(None, "chain", "cross", None),
            P(None, "chain", "cross", None),
        ),
        out_specs=P("chain", "cross", None),
        check_vma=False,
    )
```

profile of v0, /device:TPU:1, one launch (start us, length us, event | category | flops | bytes accessed | tf_op | source)
XLA Modules:
  0.0 539.7 jit_solution(4165311589859038631)
XLA Ops:
  7.3 37.0 %all-gather.18.cloned.1.call-done = bf16[1,1024,512]{2,1,0:T(8,128)(2,1)} async-done(((bf16[1,128,512]{2,1,0:T(8,128)(2,1)}), bf16[1,1024,512]{2,1,0:T(8,128)(2,1)}) %all-gather.18.cloned.1.call-update) | async-done | bytes 1048592 | tf_op jit(solution)/shard_map/all_gather | solution.py:27
  44.3 3.2 collective-permute-start
  50.4 19.6 %collective-permute-done = bf16[1024,512]{1,0:T(8,128)(2,1)S(1)} collective-permute-done((bf16[1024,512]{1,0:T(8,128)(2,1)}, bf16[1024,512]{1,0:T(8,128)(2,1)S(1)}, u32[]{:S(2)}, u32[]{:S(2)}) %collective-permute-start) | collective-permute-done | bytes 1048608 | tf_op jit(solution)/shard_map/ppermute | solution.py:10
  70.3 3.4 collective-permute-done.1
  73.8 1.9 fusion
  75.8 30.0 %all-gather.8.cloned.1.call-done = bf16[1024,512]{1,0:T(8,128)(2,1)} async-done(((bf16[128,512]{1,0:T(8,128)(2,1)}), bf16[1024,512]{1,0:T(8,128)(2,1)}) %all-gather.8.cloned.1.call-update) | async-done | bytes 1048592 | tf_op jit(solution)/shard_map/all_gather | solution.py:27
  105.8 4.2 collective-permute-start.2
  111.4 1.7 fusion.29
  113.1 19.6 %collective-permute-done.2 = bf16[1024,512]{1,0:T(8,128)(2,1)S(1)} collective-permute-done((bf16[1024,512]{1,0:T(8,128)(2,1)}, bf16[1024,512]{1,0:T(8,128)(2,1)S(1)}, u32[]{:S(2)}, u32[]{:S(2)}) %collective-permute-start.2) | collective-permute-done | bytes 1048608 | tf_op jit(solution)/shard_map/ppermute | solution.py:10
  133.1 30.1 %collective-permute-done.3 = bf16[1024,512]{1,0:T(8,128)(2,1)S(1)} collective-permute-done((bf16[1024,512]{1,0:T(8,128)(2,1)}, bf16[1024,512]{1,0:T(8,128)(2,1)S(1)}, u32[]{:S(2)}, u32[]{:S(2)}) %collective-permute-start.3) | collective-permute-done | bytes 1048608 | tf_op jit(solution)/shard_map/ppermute | solution.py:10
  163.2 2.1 fusion.10
  165.4 25.3 %all-gather.10.cloned.1.call-done = bf16[1024,512]{0,1:T(8,128)(2,1)} async-done(((bf16[128,512]{0,1:T(8,128)(2,1)}), bf16[1024,512]{0,1:T(8,128)(2,1)}) %all-gather.10.cloned.1.call-update) | async-done | bytes 1048592 | tf_op jit(solution)/shard_map/all_gather | solution.py:27
  190.7 7.8 %collective-permute-start.4 = (bf16[1024,512]{0,1:T(8,128)(2,1)}, bf16[1024,512]{0,1:T(8,128)(2,1)S(1)}, u32[]{:S(2)}, u32[]{:S(2)}) collective-permute-start(bf16[1024,512]{0,1:T(8,128)(2,1)} %all-gather.10.cloned.1.call-done), channel_id=1, source_target_pairs={{0,32},{8,40},{16,48},{24,56},{32,64},{40,72},{48,80},{56,88},{64,... | collective-permute-start | bytes 3145736 | tf_op jit(solution)/shard_map/ppermute | solution.py:10
  199.8 1.7 fusion.25
  201.4 65.5 %collective-permute-done.4 = bf16[1024,512]{0,1:T(8,128)(2,1)S(1)} collective-permute-done((bf16[1024,512]{0,1:T(8,128)(2,1)}, bf16[1024,512]{0,1:T(8,128)(2,1)S(1)}, u32[]{:S(2)}, u32[]{:S(2)}) %collective-permute-start.4) | collective-permute-done | bytes 1048608 | tf_op jit(solution)/shard_map/ppermute | solution.py:10
  267.4 2.0 fusion.9
  269.5 54.1 %all-gather.12.cloned.1.call-done = bf16[1024,512]{0,1:T(8,128)(2,1)} async-done(((bf16[128,512]{0,1:T(8,128)(2,1)}), bf16[1024,512]{0,1:T(8,128)(2,1)}) %all-gather.12.cloned.1.call-update) | async-done | bytes 1048592 | tf_op jit(solution)/shard_map/all_gather | solution.py:27
  323.7 3.2 collective-permute-start.6
  329.8 19.5 %collective-permute-done.6 = bf16[1024,512]{0,1:T(8,128)(2,1)S(1)} collective-permute-done((bf16[1024,512]{0,1:T(8,128)(2,1)}, bf16[1024,512]{0,1:T(8,128)(2,1)S(1)}, u32[]{:S(2)}, u32[]{:S(2)}) %collective-permute-start.6) | collective-permute-done | bytes 1048608 | tf_op jit(solution)/shard_map/ppermute | solution.py:10
  349.8 3.3 collective-permute-done.7
  353.1 2.0 fusion.8
  355.2 31.2 %all-gather.14.cloned.1.call-done = bf16[1024,512]{0,1:T(8,128)(2,1)} async-done(((bf16[128,512]{0,1:T(8,128)(2,1)}), bf16[1024,512]{0,1:T(8,128)(2,1)}) %all-gather.14.cloned.1.call-update) | async-done | bytes 1048592 | tf_op jit(solution)/shard_map/all_gather | solution.py:27
  386.4 4.1 collective-permute-start.8
  391.8 1.7 fusion.17
  393.5 19.6 %collective-permute-done.8 = bf16[1024,512]{0,1:T(8,128)(2,1)S(1)} collective-permute-done((bf16[1024,512]{0,1:T(8,128)(2,1)}, bf16[1024,512]{0,1:T(8,128)(2,1)S(1)}, u32[]{:S(2)}, u32[]{:S(2)}) %collective-permute-start.8) | collective-permute-done | bytes 1048608 | tf_op jit(solution)/shard_map/ppermute | solution.py:10
  413.5 28.4 %collective-permute-done.9 = bf16[1024,512]{0,1:T(8,128)(2,1)S(1)} collective-permute-done((bf16[1024,512]{0,1:T(8,128)(2,1)}, bf16[1024,512]{0,1:T(8,128)(2,1)S(1)}, u32[]{:S(2)}, u32[]{:S(2)}) %collective-permute-start.9) | collective-permute-done | bytes 1048608 | tf_op jit(solution)/shard_map/ppermute | solution.py:10
  441.9 2.0 fusion.7
  444.0 28.5 %all-gather.16.cloned.1.call-done = bf16[1024,512]{0,1:T(8,128)(2,1)} async-done(((bf16[128,512]{0,1:T(8,128)(2,1)}), bf16[1024,512]{0,1:T(8,128)(2,1)}) %all-gather.16.cloned.1.call-update) | async-done | bytes 1048592 | tf_op jit(solution)/shard_map/all_gather | solution.py:27
  472.5 7.1 %collective-permute-start.10 = (bf16[1024,512]{0,1:T(8,128)(2,1)}, bf16[1024,512]{0,1:T(8,128)(2,1)S(1)}, u32[]{:S(2)}, u32[]{:S(2)}) collective-permute-start(bf16[1024,512]{0,1:T(8,128)(2,1)} %all-gather.16.cloned.1.call-done), channel_id=1, source_target_pairs={{0,256},{8,264},{16,272},{24,280},{32,288},{40,296},{48,304},{56,3... | collective-permute-start | bytes 3145736 | tf_op jit(solution)/shard_map/ppermute | solution.py:10
  481.0 1.7 fusion.13
  482.6 32.1 %collective-permute-done.10 = bf16[1024,512]{0,1:T(8,128)(2,1)S(1)} collective-permute-done((bf16[1024,512]{0,1:T(8,128)(2,1)}, bf16[1024,512]{0,1:T(8,128)(2,1)S(1)}, u32[]{:S(2)}, u32[]{:S(2)}) %collective-permute-start.10) | collective-permute-done | bytes 1048608 | tf_op jit(solution)/shard_map/ppermute | solution.py:10
  515.1 15.6 %collective-permute-done.11 = bf16[1024,512]{0,1:T(8,128)(2,1)S(1)} collective-permute-done((bf16[1024,512]{0,1:T(8,128)(2,1)}, bf16[1024,512]{0,1:T(8,128)(2,1)S(1)}, u32[]{:S(2)}, u32[]{:S(2)}) %collective-permute-start.11) | collective-permute-done | bytes 1048608 | tf_op jit(solution)/shard_map/ppermute | solution.py:10
  (33 shorter events, 16.8 us)
Async XLA Ops:
  6.5 63.5 %copy-start = (bf16[6,1,128,1024]{3,2,1,0:T(8,128)(2,1)S(1)}, bf16[6,1,128,1024]{3,2,1,0:T(8,128)(2,1)}, u32[]{:S(2)}) copy-start(bf16[6,1,128,1024]{3,2,1,0:T(8,128)(2,1)} %param.6) | copy-start | bytes 4718596
  6.5 37.8 %all-gather.18.cloned.1.call-start = ((), (), s32[]{:S(2)}) async-start(), calls=%async_computation.5 | async-start | bytes 1179648 | tf_op jit(solution)/shard_map/all_gather | solution.py:27
  7.3 98.6 %all-gather.8.cloned.1.call-start = ((), (), s32[]{:S(2)}) async-start(), calls=%async_computation | async-start | bytes 1179648 | tf_op jit(solution)/shard_map/all_gather | solution.py:27
  44.3 25.7 %collective-permute-start = (bf16[1024,512]{1,0:T(8,128)(2,1)}, bf16[1024,512]{1,0:T(8,128)(2,1)S(1)}, u32[]{:S(2)}, u32[]{:S(2)}) collective-permute-start(bf16[1024,512]{1,0:T(8,128)(2,1)} %bitcast.86), channel_id=1, source_target_pairs={{0,8},{8,16},{16,24},{24,32},{32,40},{40,48},{48,56},{56,64},{64,7... | collective-permute-start | bytes 3145736 | tf_op jit(solution)/shard_map/ppermute | solution.py:10
  47.5 26.3 %collective-permute-start.1 = (bf16[1024,512]{1,0:T(8,128)(2,1)}, bf16[1024,512]{1,0:T(8,128)(2,1)S(1)}, u32[]{:S(2)}, u32[]{:S(2)}) collective-permute-start(bf16[1024,512]{1,0:T(8,128)(2,1)} %bitcast.87), channel_id=1, source_target_pairs={{8,0},{16,8},{24,16},{32,24},{40,32},{48,40},{56,48},{64,56},{72,6... | collective-permute-start | bytes 3145736 | tf_op jit(solution)/shard_map/ppermute | solution.py:10
  50.4 61.0 %copy-start.1 = (bf16[6,1,128,1024]{3,2,1,0:T(8,128)(2,1)S(1)}, bf16[6,1,128,1024]{3,2,1,0:T(8,128)(2,1)}, u32[]{:S(2)}) copy-start(bf16[6,1,128,1024]{3,2,1,0:T(8,128)(2,1)} %param.5) | copy-start | bytes 4718596
  75.7 115.0 %all-gather.10.cloned.1.call-start = ((), (), s32[]{:S(2)}) async-start(), calls=%async_computation.1 | async-start | bytes 1179648 | tf_op jit(solution)/shard_map/all_gather | solution.py:27
  105.8 26.8 %collective-permute-start.2 = (bf16[1024,512]{1,0:T(8,128)(2,1)}, bf16[1024,512]{1,0:T(8,128)(2,1)S(1)}, u32[]{:S(2)}, u32[]{:S(2)}) collective-permute-start(bf16[1024,512]{1,0:T(8,128)(2,1)} %all-gather.8.cloned.1.call-done), channel_id=1, source_target_pairs={{0,16},{8,24},{16,32},{24,40},{32,48},{40,56},{48,64},{56,72},{64,... | collective-permute-start | bytes 3145736 | tf_op jit(solution)/shard_map/ppermute | solution.py:10
  110.1 53.2 %collective-permute-start.3 = (bf16[1024,512]{1,0:T(8,128)(2,1)}, bf16[1024,512]{1,0:T(8,128)(2,1)S(1)}, u32[]{:S(2)}, u32[]{:S(2)}) collective-permute-start(bf16[1024,512]{1,0:T(8,128)(2,1)} %all-gather.8.cloned.1.call-done), channel_id=1, source_target_pairs={{16,0},{24,8},{32,16},{40,24},{48,32},{56,40},{64,48},{72,56},{80,... | collective-permute-start | bytes 3145736 | tf_op jit(solution)/shard_map/ppermute | solution.py:10
  165.3 158.3 %all-gather.12.cloned.1.call-start = ((), (), s32[]{:S(2)}) async-start(), calls=%async_computation.2 | async-start | bytes 1179648 | tf_op jit(solution)/shard_map/all_gather | solution.py:27
  190.7 76.3 %collective-permute-start.4 = (bf16[1024,512]{0,1:T(8,128)(2,1)}, bf16[1024,512]{0,1:T(8,128)(2,1)S(1)}, u32[]{:S(2)}, u32[]{:S(2)}) collective-permute-start(bf16[1024,512]{0,1:T(8,128)(2,1)} %all-gather.10.cloned.1.call-done), channel_id=1, source_target_pairs={{0,32},{8,40},{16,48},{24,56},{32,64},{40,72},{48,80},{56,88},{64,... | collective-permute-start | bytes 3145736 | tf_op jit(solution)/shard_map/ppermute | solution.py:10
  198.5 69.0 %collective-permute-start.5 = (bf16[1024,512]{0,1:T(8,128)(2,1)}, bf16[1024,512]{0,1:T(8,128)(2,1)S(1)}, u32[]{:S(2)}, u32[]{:S(2)}) collective-permute-start(bf16[1024,512]{0,1:T(8,128)(2,1)} %all-gather.10.cloned.1.call-done), channel_id=1, source_target_pairs={{32,0},{40,8},{48,16},{56,24},{64,32},{72,40},{80,48},{88,56},{96,... | collective-permute-start | bytes 3145736 | tf_op jit(solution)/shard_map/ppermute | solution.py:10
  269.5 116.9 %all-gather.14.cloned.1.call-start = ((), (), s32[]{:S(2)}) async-start(), calls=%async_computation.3 | async-start | bytes 1179648 | tf_op jit(solution)/shard_map/all_gather | solution.py:27
  323.7 25.7 %collective-permute-start.6 = (bf16[1024,512]{0,1:T(8,128)(2,1)}, bf16[1024,512]{0,1:T(8,128)(2,1)S(1)}, u32[]{:S(2)}, u32[]{:S(2)}) collective-permute-start(bf16[1024,512]{0,1:T(8,128)(2,1)} %all-gather.12.cloned.1.call-done), channel_id=1, source_target_pairs={{0,64},{8,72},{16,80},{24,88},{32,96},{40,104},{48,112},{56,120},{... | collective-permute-start | bytes 3145736 | tf_op jit(solution)/shard_map/ppermute | solution.py:10
  326.8 26.3 %collective-permute-start.7 = (bf16[1024,512]{0,1:T(8,128)(2,1)}, bf16[1024,512]{0,1:T(8,128)(2,1)S(1)}, u32[]{:S(2)}, u32[]{:S(2)}) collective-permute-start(bf16[1024,512]{0,1:T(8,128)(2,1)} %all-gather.12.cloned.1.call-done), channel_id=1, source_target_pairs={{64,0},{72,8},{80,16},{88,24},{96,32},{104,40},{112,48},{120,56},{... | collective-permute-start | bytes 3145736 | tf_op jit(solution)/shard_map/ppermute | solution.py:10
  355.2 117.4 %all-gather.16.cloned.1.call-start = ((), (), s32[]{:S(2)}) async-start(), calls=%async_computation.4 | async-start | bytes 1179648 | tf_op jit(solution)/shard_map/all_gather | solution.py:27
  386.4 26.6 %collective-permute-start.8 = (bf16[1024,512]{0,1:T(8,128)(2,1)}, bf16[1024,512]{0,1:T(8,128)(2,1)S(1)}, u32[]{:S(2)}, u32[]{:S(2)}) collective-permute-start(bf16[1024,512]{0,1:T(8,128)(2,1)} %all-gather.14.cloned.1.call-done), channel_id=1, source_target_pairs={{0,128},{8,136},{16,144},{24,152},{32,160},{40,168},{48,176},{56,1... | collective-permute-start | bytes 3145736 | tf_op jit(solution)/shard_map/ppermute | solution.py:10
  390.5 51.5 %collective-permute-start.9 = (bf16[1024,512]{0,1:T(8,128)(2,1)}, bf16[1024,512]{0,1:T(8,128)(2,1)S(1)}, u32[]{:S(2)}, u32[]{:S(2)}) collective-permute-start(bf16[1024,512]{0,1:T(8,128)(2,1)} %all-gather.14.cloned.1.call-done), channel_id=1, source_target_pairs={{128,0},{136,8},{144,16},{152,24},{160,32},{168,40},{176,48},{184,... | collective-permute-start | bytes 3145736 | tf_op jit(solution)/shard_map/ppermute | solution.py:10
  472.5 42.2 %collective-permute-start.10 = (bf16[1024,512]{0,1:T(8,128)(2,1)}, bf16[1024,512]{0,1:T(8,128)(2,1)S(1)}, u32[]{:S(2)}, u32[]{:S(2)}) collective-permute-start(bf16[1024,512]{0,1:T(8,128)(2,1)} %all-gather.16.cloned.1.call-done), channel_id=1, source_target_pairs={{0,256},{8,264},{16,272},{24,280},{32,288},{40,296},{48,304},{56,3... | collective-permute-start | bytes 3145736 | tf_op jit(solution)/shard_map/ppermute | solution.py:10
  479.7 51.0 %collective-permute-start.11 = (bf16[1024,512]{0,1:T(8,128)(2,1)}, bf16[1024,512]{0,1:T(8,128)(2,1)S(1)}, u32[]{:S(2)}, u32[]{:S(2)}) collective-permute-start(bf16[1024,512]{0,1:T(8,128)(2,1)} %all-gather.16.cloned.1.call-done), channel_id=1, source_target_pairs={{256,0},{264,8},{272,16},{280,24},{288,32},{296,40},{304,48},{312,... | collective-permute-start | bytes 3145736 | tf_op jit(solution)/shard_map/ppermute | solution.py:10
Sparse Core Ops, SparseCore 0:
  9.5 34.7 all-gather.17
  75.8 29.9 all-gather.7
  165.5 25.1 all-gather.9
  269.6 53.9 all-gather.11
  355.3 31.0 all-gather.13
  444.1 28.3 all-gather.15
where the time goes:
time: 540 us
  waiting for transfers between devices  464 us (86%)
  starting transfers between devices  37.5 us (7%)
  matrix products  24.1 us (4%)
  between operations  13.7 us (3%)
    ppermute x12, waiting for transfers between devices, shifted(): lax.ppermute(value, axis, [(source, source + steps) for source in range(i...  257 us
    all_gather x6, waiting for transfers between devices, body(): whole = lax.all_gather(current, 'cross', axis=0, tiled=True)  206 us
    ppermute x12, starting transfers between devices, shifted(): lax.ppermute(value, axis, [(source, source + steps) for source in range(i...  37.3 us
    dot_general x6, matrix products, body(): total = total - jnp.dot(up_mat, upper, preferred_element_type=jnp.float32)  11.5 us
  transfers between devices with their start and end apart: 18, of which 17 were waited for; matrix products, arithmetic and copies ran while one was open for 2% of the time, Pallas kernels for 0%

commit v1 on v0

--- a/solution.py
+++ b/solution.py
@@ -24,7 +24,9 @@
         own_mat = self_factor[level, 0]
         low_mat = lower_factor[level, 0]
         up_mat = upper_factor[level, 0]
-        whole = lax.all_gather(current, "cross", axis=0, tiled=True)
+        whole = jnp.concatenate(
+            lax.all_to_all(jnp.stack([current] * lax.axis_size("cross")), "cross", 0, 0), axis=0
+        )
         lower, upper = reach_full(whole, dist)
         total = jnp.dot(own_mat, whole, preferred_element_type=jnp.float32)
         total = total - jnp.dot(low_mat, lower, preferred_element_type=jnp.float32)

time: 540 us -> 454 us (0.84)
  waiting for transfers between devices: 464 us -> 248 us
  blocking collectives: 0 us -> 124 us
  starting transfers between devices: 37.5 us -> 61.8 us
  between operations: 13.7 us -> 0.29 us
  matrix products: 24.1 us -> 13.8 us
    all_gather x6 -> x0, waiting for transfers between devices: 206 us -> none  [body(): whole = lax.all_gather(current, 'cross', axis=0, tiled=True)]
    all_to_all x0 -> x6, blocking collectives: none -> 124 us  [body(): lax.all_to_all(jnp.stack([current] * lax.axis_size('cross')), 'cross', 0, 0)]
    ppermute x12, starting transfers between devices: 37.3 us -> 61.8 us  [shifted(): lax.ppermute(value, axis, [(source, source + steps) for source in range(i...]
    ppermute x12, waiting for transfers between devices: 257 us -> 248 us  [shifted(): lax.ppermute(value, axis, [(source, source + steps) for source in range(i...]
    dot_general x6, matrix products: 9.96 us -> 2.69 us  [body(): total = jnp.dot(own_mat, whole, preferred_element_type=jnp.float32)]
  transfers between devices with their start and end apart: 18 -> 12, of which waited for: 17 -> 11; matrix products, arithmetic and copies ran while one was open for 2% -> 1% of each run, Pallas kernels for 0% -> 0%
where the time goes in v1:
time: 454 us; the launch traced here: 451 us
  waiting for transfers between devices  248 us (55%)
  blocking collectives  124 us (27%)
  starting transfers between devices  61.8 us (14%)
  matrix products  13.8 us (3%)
    ppermute x12, waiting for transfers between devices, shifted(): lax.ppermute(value, axis, [(source, source + steps) for source in range(i...  248 us
    all_to_all x6, blocking collectives, body(): lax.all_to_all(jnp.stack([current] * lax.axis_size('cross')), 'cross', 0, 0)  124 us
    ppermute x12, starting transfers between devices, shifted(): lax.ppermute(value, axis, [(source, source + steps) for source in range(i...  61.8 us
  transfers between devices with their start and end apart: 12, of which 11 were waited for; matrix products, arithmetic and copies ran while one was open for 1% of the time, Pallas kernels for 0%

profile of v1, /device:TPU:1, one launch (start us, length us, event | category | flops | bytes accessed | tf_op | source)
XLA Modules:
  0.0 450.7 jit_solution(2460205022453889421)
XLA Ops:
  1.1 24.5 %all_to_all.30 = bf16[8,128,512]{2,1,0:T(8,128)(2,1)S(1)} all-to-all(bf16[8,128,512]{2,1,0:T(8,128)(2,1)S(1)} %stack.12), channel_id=1, replica_groups=mesh['chain'=64,'cross'=8] {'cross'}, dimensions={0} | all-to-all | bytes 2097152 | tf_op jit(solution)/shard_map/all_to_all | solution.py:28
  25.6 1.3 collective-permute-start
  27.0 1.3 collective-permute-start.1
  28.6 20.0 %collective-permute-done = bf16[1024,512]{1,0:T(8,128)(2,1)S(1)} collective-permute-done((bf16[1024,512]{1,0:T(8,128)(2,1)S(1)}, bf16[1024,512]{1,0:T(8,128)(2,1)S(1)}, u32[]{:S(2)}, u32[]{:S(2)}) %collective-permute-start) | collective-permute-done | bytes 1048608 | tf_op jit(solution)/shard_map/ppermute | solution.py:10
  48.9 3.5 collective-permute-done.1
  53.8 19.4 %all_to_all.31 = bf16[8,128,512]{2,1,0:T(8,128)(2,1)S(1)} all-to-all(bf16[8,128,512]{2,1,0:T(8,128)(2,1)S(1)} %stack.13), channel_id=1, replica_groups=mesh['chain'=64,'cross'=8] {'cross'}, dimensions={0} | all-to-all | bytes 2097152 | tf_op jit(solution)/shard_map/all_to_all | solution.py:28
  73.3 6.7 %collective-permute-start.2 = (bf16[1024,512]{1,0:T(8,128)(2,1)S(1)}, bf16[1024,512]{1,0:T(8,128)(2,1)S(1)}, u32[]{:S(2)}, u32[]{:S(2)}) collective-permute-start(bf16[1024,512]{1,0:T(8,128)(2,1)S(1)} %bitcast.94), channel_id=1, source_target_pairs={{0,16},{8,24},{16,32},{24,40},{32,48},{40,56},{48,64},{56,72},{64,... | collective-permute-start | bytes 3145736 | tf_op jit(solution)/shard_map/ppermute | solution.py:10
  79.9 1.3 collective-permute-start.3
  81.7 19.6 %collective-permute-done.2 = bf16[1024,512]{1,0:T(8,128)(2,1)S(1)} collective-permute-done((bf16[1024,512]{1,0:T(8,128)(2,1)S(1)}, bf16[1024,512]{1,0:T(8,128)(2,1)S(1)}, u32[]{:S(2)}, u32[]{:S(2)}) %collective-permute-start.2) | collective-permute-done | bytes 1048608 | tf_op jit(solution)/shard_map/ppermute | solution.py:10
  101.8 25.2 %collective-permute-done.3 = bf16[1024,512]{1,0:T(8,128)(2,1)S(1)} collective-permute-done((bf16[1024,512]{1,0:T(8,128)(2,1)S(1)}, bf16[1024,512]{1,0:T(8,128)(2,1)S(1)}, u32[]{:S(2)}, u32[]{:S(2)}) %collective-permute-start.3) | collective-permute-done | bytes 1048608 | tf_op jit(solution)/shard_map/ppermute | solution.py:10
  127.0 1.4 fusion.10
  128.6 21.5 %all_to_all.32 = bf16[8,128,512]{2,1,0:T(8,128)(2,1)S(1)} all-to-all(bf16[8,128,512]{2,1,0:T(8,128)(2,1)S(1)} %stack.14), channel_id=1, replica_groups=mesh['chain'=64,'cross'=8] {'cross'}, dimensions={0} | all-to-all | bytes 2097152 | tf_op jit(solution)/shard_map/all_to_all | solution.py:28
  150.1 5.9 %collective-permute-start.4 = (bf16[1024,512]{1,0:T(8,128)(2,1)S(1)}, bf16[1024,512]{1,0:T(8,128)(2,1)S(1)}, u32[]{:S(2)}, u32[]{:S(2)}) collective-permute-start(bf16[1024,512]{1,0:T(8,128)(2,1)S(1)} %bitcast.97), channel_id=1, source_target_pairs={{0,32},{8,40},{16,48},{24,56},{32,64},{40,72},{48,80},{56,88},{64,... | collective-permute-start | bytes 3145736 | tf_op jit(solution)/shard_map/ppermute | solution.py:10
  156.0 1.3 collective-permute-start.5
  157.8 66.8 %collective-permute-done.4 = bf16[1024,512]{1,0:T(8,128)(2,1)S(1)} collective-permute-done((bf16[1024,512]{1,0:T(8,128)(2,1)S(1)}, bf16[1024,512]{1,0:T(8,128)(2,1)S(1)}, u32[]{:S(2)}, u32[]{:S(2)}) %collective-permute-start.4) | collective-permute-done | bytes 1048608 | tf_op jit(solution)/shard_map/ppermute | solution.py:10
  225.0 1.4 fusion.9
  226.7 19.4 %all_to_all.33 = bf16[8,128,512]{2,1,0:T(8,128)(2,1)S(1)} all-to-all(bf16[8,128,512]{2,1,0:T(8,128)(2,1)S(1)} %stack.15), channel_id=1, replica_groups=mesh['chain'=64,'cross'=8] {'cross'}, dimensions={0} | all-to-all | bytes 2097152 | tf_op jit(solution)/shard_map/all_to_all | solution.py:28
  246.1 24.4 %collective-permute-start.6 = (bf16[1024,512]{1,0:T(8,128)(2,1)S(1)}, bf16[1024,512]{1,0:T(8,128)(2,1)S(1)}, u32[]{:S(2)}, u32[]{:S(2)}) collective-permute-start(bf16[1024,512]{1,0:T(8,128)(2,1)S(1)} %bitcast.100), channel_id=1, source_target_pairs={{0,64},{8,72},{16,80},{24,88},{32,96},{40,104},{48,112},{56,120},{... | collective-permute-start | bytes 3145736 | tf_op jit(solution)/shard_map/ppermute | solution.py:10
  270.5 1.3 collective-permute-start.7
  272.3 19.5 %collective-permute-done.6 = bf16[1024,512]{1,0:T(8,128)(2,1)S(1)} collective-permute-done((bf16[1024,512]{1,0:T(8,128)(2,1)S(1)}, bf16[1024,512]{1,0:T(8,128)(2,1)S(1)}, u32[]{:S(2)}, u32[]{:S(2)}) %collective-permute-start.6) | collective-permute-done | bytes 1048608 | tf_op jit(solution)/shard_map/ppermute | solution.py:10
  292.3 3.4 collective-permute-done.7
  295.8 1.4 fusion.8
  297.4 19.7 %all_to_all.34 = bf16[8,128,512]{2,1,0:T(8,128)(2,1)S(1)} all-to-all(bf16[8,128,512]{2,1,0:T(8,128)(2,1)S(1)} %stack.16), channel_id=1, replica_groups=mesh['chain'=64,'cross'=8] {'cross'}, dimensions={0} | all-to-all | bytes 2097152 | tf_op jit(solution)/shard_map/all_to_all | solution.py:28
  317.1 10.5 %collective-permute-start.8 = (bf16[1024,512]{1,0:T(8,128)(2,1)S(1)}, bf16[1024,512]{1,0:T(8,128)(2,1)S(1)}, u32[]{:S(2)}, u32[]{:S(2)}) collective-permute-start(bf16[1024,512]{1,0:T(8,128)(2,1)S(1)} %bitcast.103), channel_id=1, source_target_pairs={{0,128},{8,136},{16,144},{24,152},{32,160},{40,168},{48,176},{56,1... | collective-permute-start | bytes 3145736 | tf_op jit(solution)/shard_map/ppermute | solution.py:10
  329.4 19.6 %collective-permute-done.8 = bf16[1024,512]{1,0:T(8,128)(2,1)S(1)} collective-permute-done((bf16[1024,512]{1,0:T(8,128)(2,1)S(1)}, bf16[1024,512]{1,0:T(8,128)(2,1)S(1)}, u32[]{:S(2)}, u32[]{:S(2)}) %collective-permute-start.8) | collective-permute-done | bytes 1048608 | tf_op jit(solution)/shard_map/ppermute | solution.py:10
  349.5 23.4 %collective-permute-done.9 = bf16[1024,512]{1,0:T(8,128)(2,1)S(1)} collective-permute-done((bf16[1024,512]{1,0:T(8,128)(2,1)S(1)}, bf16[1024,512]{1,0:T(8,128)(2,1)S(1)}, u32[]{:S(2)}, u32[]{:S(2)}) %collective-permute-start.9) | collective-permute-done | bytes 1048608 | tf_op jit(solution)/shard_map/ppermute | solution.py:10
  372.8 1.4 fusion.7
  374.5 19.7 %all_to_all.35 = bf16[8,128,512]{2,1,0:T(8,128)(2,1)S(1)} all-to-all(bf16[8,128,512]{2,1,0:T(8,128)(2,1)S(1)} %stack.17), channel_id=1, replica_groups=mesh['chain'=64,'cross'=8] {'cross'}, dimensions={0} | all-to-all | bytes 2097152 | tf_op jit(solution)/shard_map/all_to_all | solution.py:28
  394.2 5.3 %collective-permute-start.10 = (bf16[1024,512]{1,0:T(8,128)(2,1)S(1)}, bf16[1024,512]{1,0:T(8,128)(2,1)S(1)}, u32[]{:S(2)}, u32[]{:S(2)}) collective-permute-start(bf16[1024,512]{1,0:T(8,128)(2,1)S(1)} %bitcast.106), channel_id=1, source_target_pairs={{0,256},{8,264},{16,272},{24,280},{32,288},{40,296},{48,304},{56,3... | collective-permute-start | bytes 3145736 | tf_op jit(solution)/shard_map/ppermute | solution.py:10
  401.3 42.4 %collective-permute-done.10 = bf16[1024,512]{1,0:T(8,128)(2,1)S(1)} collective-permute-done((bf16[1024,512]{1,0:T(8,128)(2,1)S(1)}, bf16[1024,512]{1,0:T(8,128)(2,1)S(1)}, u32[]{:S(2)}, u32[]{:S(2)}) %collective-permute-start.10) | collective-permute-done | bytes 1048608 | tf_op jit(solution)/shard_map/ppermute | solution.py:10
  444.1 4.4 collective-permute-done.11
  448.5 1.4 fusion.6
  (31 shorter events, 12.0 us)
Async XLA Ops:
  0.0 28.3 %copy-start.1 = (bf16[6,1,128,1024]{3,2,1,0:T(8,128)(2,1)S(1)}, bf16[6,1,128,1024]{3,2,1,0:T(8,128)(2,1)}, u32[]{:S(2)}) copy-start(bf16[6,1,128,1024]{3,2,1,0:T(8,128)(2,1)} %param.5) | copy-start | bytes 4718596
  1.1 47.5 %copy-start = (bf16[6,1,128,1024]{3,2,1,0:T(8,128)(2,1)S(1)}, bf16[6,1,128,1024]{3,2,1,0:T(8,128)(2,1)}, u32[]{:S(2)}) copy-start(bf16[6,1,128,1024]{3,2,1,0:T(8,128)(2,1)} %param.6) | copy-start | bytes 4718596
  25.6 23.0 %collective-permute-start = (bf16[1024,512]{1,0:T(8,128)(2,1)S(1)}, bf16[1024,512]{1,0:T(8,128)(2,1)S(1)}, u32[]{:S(2)}, u32[]{:S(2)}) collective-permute-start(bf16[1024,512]{1,0:T(8,128)(2,1)S(1)} %bitcast.91), channel_id=1, source_target_pairs={{0,8},{8,16},{16,24},{24,32},{32,40},{40,48},{48,56},{56,64},{64,7... | collective-permute-start | bytes 3145736 | tf_op jit(solution)/shard_map/ppermute | solution.py:10
  27.0 25.5 %collective-permute-start.1 = (bf16[1024,512]{1,0:T(8,128)(2,1)S(1)}, bf16[1024,512]{1,0:T(8,128)(2,1)S(1)}, u32[]{:S(2)}, u32[]{:S(2)}) collective-permute-start(bf16[1024,512]{1,0:T(8,128)(2,1)S(1)} %bitcast.92), channel_id=1, source_target_pairs={{8,0},{16,8},{24,16},{32,24},{40,32},{48,40},{56,48},{64,56},{72,6... | collective-permute-start | bytes 3145736 | tf_op jit(solution)/shard_map/ppermute | solution.py:10
  73.3 28.0 %collective-permute-start.2 = (bf16[1024,512]{1,0:T(8,128)(2,1)S(1)}, bf16[1024,512]{1,0:T(8,128)(2,1)S(1)}, u32[]{:S(2)}, u32[]{:S(2)}) collective-permute-start(bf16[1024,512]{1,0:T(8,128)(2,1)S(1)} %bitcast.94), channel_id=1, source_target_pairs={{0,16},{8,24},{16,32},{24,40},{32,48},{40,56},{48,64},{56,72},{64,... | collective-permute-start | bytes 3145736 | tf_op jit(solution)/shard_map/ppermute | solution.py:10
  79.9 47.0 %collective-permute-start.3 = (bf16[1024,512]{1,0:T(8,128)(2,1)S(1)}, bf16[1024,512]{1,0:T(8,128)(2,1)S(1)}, u32[]{:S(2)}, u32[]{:S(2)}) collective-permute-start(bf16[1024,512]{1,0:T(8,128)(2,1)S(1)} %bitcast.95), channel_id=1, source_target_pairs={{16,0},{24,8},{32,16},{40,24},{48,32},{56,40},{64,48},{72,56},{80,... | collective-permute-start | bytes 3145736 | tf_op jit(solution)/shard_map/ppermute | solution.py:10
  150.1 74.4 %collective-permute-start.4 = (bf16[1024,512]{1,0:T(8,128)(2,1)S(1)}, bf16[1024,512]{1,0:T(8,128)(2,1)S(1)}, u32[]{:S(2)}, u32[]{:S(2)}) collective-permute-start(bf16[1024,512]{1,0:T(8,128)(2,1)S(1)} %bitcast.97), channel_id=1, source_target_pairs={{0,32},{8,40},{16,48},{24,56},{32,64},{40,72},{48,80},{56,88},{64,... | collective-permute-start | bytes 3145736 | tf_op jit(solution)/shard_map/ppermute | solution.py:10
  156.0 69.0 %collective-permute-start.5 = (bf16[1024,512]{1,0:T(8,128)(2,1)S(1)}, bf16[1024,512]{1,0:T(8,128)(2,1)S(1)}, u32[]{:S(2)}, u32[]{:S(2)}) collective-permute-start(bf16[1024,512]{1,0:T(8,128)(2,1)S(1)} %bitcast.98), channel_id=1, source_target_pairs={{32,0},{40,8},{48,16},{56,24},{64,32},{72,40},{80,48},{88,56},{96,... | collective-permute-start | bytes 3145736 | tf_op jit(solution)/shard_map/ppermute | solution.py:10
  246.1 45.7 %collective-permute-start.6 = (bf16[1024,512]{1,0:T(8,128)(2,1)S(1)}, bf16[1024,512]{1,0:T(8,128)(2,1)S(1)}, u32[]{:S(2)}, u32[]{:S(2)}) collective-permute-start(bf16[1024,512]{1,0:T(8,128)(2,1)S(1)} %bitcast.100), channel_id=1, source_target_pairs={{0,64},{8,72},{16,80},{24,88},{32,96},{40,104},{48,112},{56,120},{... | collective-permute-start | bytes 3145736 | tf_op jit(solution)/shard_map/ppermute | solution.py:10
  270.5 25.2 %collective-permute-start.7 = (bf16[1024,512]{1,0:T(8,128)(2,1)S(1)}, bf16[1024,512]{1,0:T(8,128)(2,1)S(1)}, u32[]{:S(2)}, u32[]{:S(2)}) collective-permute-start(bf16[1024,512]{1,0:T(8,128)(2,1)S(1)} %bitcast.101), channel_id=1, source_target_pairs={{64,0},{72,8},{80,16},{88,24},{96,32},{104,40},{112,48},{120,56},{... | collective-permute-start | bytes 3145736 | tf_op jit(solution)/shard_map/ppermute | solution.py:10
  317.1 31.9 %collective-permute-start.8 = (bf16[1024,512]{1,0:T(8,128)(2,1)S(1)}, bf16[1024,512]{1,0:T(8,128)(2,1)S(1)}, u32[]{:S(2)}, u32[]{:S(2)}) collective-permute-start(bf16[1024,512]{1,0:T(8,128)(2,1)S(1)} %bitcast.103), channel_id=1, source_target_pairs={{0,128},{8,136},{16,144},{24,152},{32,160},{40,168},{48,176},{56,1... | collective-permute-start | bytes 3145736 | tf_op jit(solution)/shard_map/ppermute | solution.py:10
  327.6 45.2 %collective-permute-start.9 = (bf16[1024,512]{1,0:T(8,128)(2,1)S(1)}, bf16[1024,512]{1,0:T(8,128)(2,1)S(1)}, u32[]{:S(2)}, u32[]{:S(2)}) collective-permute-start(bf16[1024,512]{1,0:T(8,128)(2,1)S(1)} %bitcast.104), channel_id=1, source_target_pairs={{128,0},{136,8},{144,16},{152,24},{160,32},{168,40},{176,48},{184,... | collective-permute-start | bytes 3145736 | tf_op jit(solution)/shard_map/ppermute | solution.py:10
  394.2 49.4 %collective-permute-start.10 = (bf16[1024,512]{1,0:T(8,128)(2,1)S(1)}, bf16[1024,512]{1,0:T(8,128)(2,1)S(1)}, u32[]{:S(2)}, u32[]{:S(2)}) collective-permute-start(bf16[1024,512]{1,0:T(8,128)(2,1)S(1)} %bitcast.106), channel_id=1, source_target_pairs={{0,256},{8,264},{16,272},{24,280},{32,288},{40,296},{48,304},{56,3... | collective-permute-start | bytes 3145736 | tf_op jit(solution)/shard_map/ppermute | solution.py:10
  399.5 49.0 %collective-permute-start.11 = (bf16[1024,512]{1,0:T(8,128)(2,1)S(1)}, bf16[1024,512]{1,0:T(8,128)(2,1)S(1)}, u32[]{:S(2)}, u32[]{:S(2)}) collective-permute-start(bf16[1024,512]{1,0:T(8,128)(2,1)S(1)} %bitcast.107), channel_id=1, source_target_pairs={{256,0},{264,8},{272,16},{280,24},{288,32},{296,40},{304,48},{312,... | collective-permute-start | bytes 3145736 | tf_op jit(solution)/shard_map/ppermute | solution.py:10
